TPU v7x, 32 devices: a whole 2x2x4 slice. The times are simulated.
32 devices in a mesh: dp: 8 (over y, x, core), fsdp: 4 (over z).
Axes of the slice: x: 2, y: 2, z: 4, core: 2. Of those that a mesh axis runs over, the one named last changes fastest.
Arguments:
- query_cache: bfloat16 [384, 1024], P('dp', 'fsdp'), may hold values from -8 to 8
- region_cache: bfloat16 [384, 1024], P('dp', 'fsdp'), may hold values from -8 to 8
- positive: int32 [384], P('dp'), may hold values from 0 to 383, each once
- hidden_states: bfloat16 [4096, 4096], P(('dp', 'fsdp')), may hold values from -12 to 12
- segment_ids: int32 [8, 512], P('dp', 'fsdp'), may hold values from 0 to 47, never falling along the last dimension, each value on 1 to 21 neighbouring positions
- norm_gain: bfloat16 [4096], replicated, may hold values from 0.099609375 to 1.8984375
- proj_weight: bfloat16 [4096, 1024], P('fsdp'), may hold values from -1 to 1
Outputs:
- mean_loss: float32 [], replicated
- query_grad: float32 [384, 1024], P('dp', 'fsdp')
- region_grad: float32 [384, 1024], P('dp', 'fsdp')
- hidden_grad: bfloat16 [4096, 4096], P(('dp', 'fsdp'))
- gain_grad: float32 [4096], replicated
- proj_grad: float32 [4096, 1024], P('dp', 'fsdp')
Inputs may be any that keep to these rules, and one draw needn't show every extreme that they name: Each region is the positive of exactly one instruction. `segment_ids`: within a pair group the ids never fall, every instruction has at least one token, and one has exactly 21.
All inputs are finite; a program needn't handle non-finite values.
Results may differ from a plain program's by a relative error of at most 0.0088.
Values may be sent and summed in bfloat16 or wider, within the bound.
No kernel may reach another device: no remote copies, remote signals or barrier semaphores. Data moves between devices by JAX's collectives and lax.ppermute only.
A program may use at most 64 MiB of HBM per device.

v0:
```python
import jax
import jax.numpy as jnp
from jax import lax
from jax.sharding import PartitionSpec as P

E = 1024
EPS = 1e-05


def local(query_cache, region_cache, positive, hidden_states, segment_ids, norm_gain, proj_weight):
    row_count = query_cache.shape[0]
    data_count = lax.axis_size("dp")
    pair_count = row_count * data_count
    logit_scale = float(E) ** (-0.5)
    contract_last = (((1,), (1,)), ((), ()))
    contract_first = (((0,), (0,)), ((), ()))
    region_all, query_all = (
        lax.all_gather(region_cache, "dp", axis=0, tiled=True),
        lax.all_gather(query_cache, "dp", axis=0, tiled=True),
    )
    partial_value = lax.dot_general(
        query_cache, region_all, contract_last, preferred_element_type=jnp.float32
    )
    scores = lax.psum(partial_value, "fsdp") * logit_scale
    row_max = jnp.max(scores, axis=1, keepdims=True)
    log_total = row_max[:, 0] + jnp.log(jnp.sum(jnp.exp(scores - row_max), axis=1))
    columns = lax.broadcasted_iota(jnp.int32, (1, pair_count), 1)
    matched = columns == positive[:, None]
    target_score = jnp.sum(jnp.where(matched, scores, jnp.zeros_like(scores)), axis=1)
    loss_local = jnp.sum(log_total - target_score)
    grad_probs = (jnp.exp(scores - log_total[:, None]) - matched.astype(jnp.float32)).astype(
        jnp.bfloat16
    )
    query_grad = logit_scale * jnp.dot(grad_probs, region_all, preferred_element_type=jnp.float32)
    totals_all, targets_all = (
        lax.all_gather(log_total, "dp", axis=0, tiled=True),
        lax.all_gather(positive.astype(jnp.float32), "dp", axis=0, tiled=True),
    )
    partial_t = lax.dot_general(
        region_cache, query_all, contract_last, preferred_element_type=jnp.float32
    )
    scores_t = lax.psum(partial_t, "fsdp") * logit_scale
    own_rows = (
        lax.axis_index("dp") * row_count + lax.broadcasted_iota(jnp.int32, (row_count, 1), 0)
    ).astype(jnp.float32)
    matched_t = targets_all[None, :] == own_rows
    probs_t = (jnp.exp(scores_t - totals_all[None, :]) - matched_t.astype(jnp.float32)).astype(
        jnp.bfloat16
    )
    region_grad = logit_scale * jnp.dot(probs_t, query_all, preferred_element_type=jnp.float32)
    gain = norm_gain.astype(jnp.float32)
    states = hidden_states.astype(jnp.float32)
    inv_rms = lax.rsqrt(jnp.mean(states * states, axis=1, keepdims=True) + EPS)
    normed = (states * inv_rms * gain).astype(jnp.bfloat16)
    labels = lax.broadcasted_iota(jnp.int32, (row_count, 1), 0)
    member = segment_ids[0][None, :] == labels
    pooled_part = jnp.dot(member.astype(jnp.bfloat16), normed, preferred_element_type=jnp.float32)
    counts_part = jnp.sum(member.astype(jnp.float32), axis=1)
    pooled, counts = lax.psum((pooled_part, counts_part), "fsdp")
    mean_pooled = (pooled / counts[:, None]).astype(jnp.bfloat16)
    grad_low = query_grad.astype(jnp.bfloat16)
    grad_full = lax.all_gather(grad_low, "fsdp", axis=1, tiled=True)
    mean_part = lax.dot_general(
        grad_full, proj_weight, contract_last, preferred_element_type=jnp.float32
    )
    mean_grad = lax.all_gather(mean_part, "fsdp", axis=1, tiled=True)
    pool_grad = mean_grad / counts[:, None]
    normed_grad = lax.dot_general(
        member.astype(jnp.float32),
        pool_grad,
        contract_first,
        precision=lax.Precision.HIGHEST,
        preferred_element_type=jnp.float32,
    )
    gain_part = jnp.sum(normed_grad * states * inv_rms, axis=0)
    scaled = gain * normed_grad
    inner = jnp.mean(scaled * states, axis=1, keepdims=True)
    hidden_grad = (inv_rms * scaled - states * inv_rms**3 * inner).astype(jnp.bfloat16)
    proj_grad = lax.psum_scatter(
        lax.dot_general(mean_pooled, grad_low, contract_first, preferred_element_type=jnp.float32),
        "dp",
        scatter_dimension=0,
        tiled=True,
    )
    loss_total = lax.psum(loss_local, "dp")
    gain_grad = lax.psum(gain_part, ("dp", "fsdp"))
    mean_loss = loss_total / pair_count
    return (mean_loss, query_grad, region_grad, hidden_grad, gain_grad, proj_grad)


def solution(mesh):
    in_specs = (
        P("dp", "fsdp"),
        P("dp", "fsdp"),
        P("dp"),
        P(("dp", "fsdp"), None),
        P("dp", "fsdp"),
        P(),
        P("fsdp", None),
    )
    out_specs = (
        P(),
        P("dp", "fsdp"),
        P("dp", "fsdp"),
        P(("dp", "fsdp"), None),
        P(),
        P("dp", "fsdp"),
    )
    return jax.shard_map(local, mesh=mesh, in_specs=in_specs, out_specs=out_specs, check_vma=False)
```

profile of v0, /device:TPU:12, one launch (start us, length us, event | category | flops | bytes accessed | tf_op | source)
XLA Modules:
  0.0 194.4 jit_solution(16001850921238040908)
XLA Ops:
  7.2 0.0 copy-start
  7.2 0.0 copy-start.1
  7.2 0.0 all-reduce.6.cloned.1.call-start
  7.2 0.0 copy-start.15
  7.2 1.7 fusion
  8.9 0.6 multiply_multiply_fusion
  9.5 0.0 copy-start.11
  9.5 0.7 convert_element_type.53
  10.2 9.2 %all_gather.19 = bf16[384,256]{1,0:T(8,128)(2,1)S(1)} all-gather(bf16[48,256]{1,0:T(8,128)(2,1)} %param.7), channel_id=1, replica_groups=mesh['dp'=8,'fsdp'=4] {'dp'}, dimensions={0}, use_global_device_ids=true | all-gather | bytes 221184 | tf_op jit(solution)/shard_map/all_gather | solution.py:19
  19.5 8.5 %all_gather.18 = bf16[384,256]{1,0:T(8,128)(2,1)S(1)} all-gather(bf16[48,256]{1,0:T(8,128)(2,1)} %param.8), channel_id=1, replica_groups=mesh['dp'=8,'fsdp'=4] {'dp'}, dimensions={0}, use_global_device_ids=true | all-gather | bytes 221184 | tf_op jit(solution)/shard_map/all_gather | solution.py:18
  27.9 1.6 fusion.32
  29.5 1.6 fusion.31
  31.0 0.0 copy-done.11
  31.0 0.0 copy-done.1
  31.1 0.0 copy-done.15
  31.1 1.4 fusion.9
  32.4 0.0 all-reduce.6.cloned.1.call-update
  32.4 0.0 reduce-scatter.2.cloned.1.call-start
  32.5 1.2 dynamic-slice
  34.4 1.3 convert_reduce_fusion
  35.7 9.7 %psum.45 = f32[48]{0:T(128)} all-reduce(f32[48]{0:T(128)} %convert_reduce_fusion), channel_id=1, replica_groups=mesh['dp'=8,'fsdp'=4] {'fsdp'}, use_global_device_ids=true, to_apply=%region_9.10 | all-reduce | flops 48 | bytes 384 | tf_op jit(solution)/shard_map/psum | solution.py:59
  45.4 37.4 %all-reduce.6.cloned.1.call-done = (f32[48,384]{1,0:T(8,128)}, f32[48,384]{1,0:T(8,128)}, f32[48,4096]{1,0:T(8,128)}) async-done(((f32[48,384]{1,0:T(8,128)}, f32[48,384]{1,0:T(8,128)}, f32[48,4096]{1,0:T(8,128)}), (f32[48,384]{1,0:T(8,128)}, f32[48,384]{1,0:T(8,128)}, f32[48,4096]{1,0:T(8,128)})) %all-reduce.6.cloned.1.call-update) | async-done | bytes 933904 | tf_op jit(solution)/shard_map/psum | solution.py:24
  82.8 1.0 multiply_reduce_fusion
  83.8 1.6 select_reduce_fusion
  85.4 0.1 fusion.29
  85.5 0.0 copy-start.5
  85.5 1.7 fusion.30
  87.2 0.0 copy-done.5
  87.2 0.0 copy-start.2
  87.2 0.0 copy-done.8
  87.2 0.6 copy-done.2
  87.9 3.9 %fusion.15 = f32[4096,256]{1,0:T(8,128)} fusion(bf16[48,256]{1,0:T(8,128)(2,1)S(1)} %get-tuple-element.20, f32[48,4096]{1,0:T(8,128)} %get-tuple-element.15, f32[48]{0:T(128)} %psum.45), kind=kOutput, calls=%fused_computation.22 | convolution fusion | flops 101056512 | bytes 5005504 | tf_op jit(solution)/shard_map/dot_general | solution.py:80
  91.7 0.0 copy-start.7
  91.7 0.0 copy-start.9
  91.8 0.0 copy-start.14
  91.8 0.0 copy-start.6
  91.8 0.0 copy-start.3
  91.8 0.0 reduce-scatter.2.cloned.1.call-update
  91.8 0.0 copy-start.12
  91.8 0.0 copy-start.13
  91.8 0.0 copy-start.16
  91.9 0.5 copy-done.7
  92.4 0.1 convert_dynamic-update-slice_fusion
  92.5 0.0 copy-done.9
  92.5 0.0 copy-done.14
  92.5 0.6 subtract_reduce_fusion
  93.1 0.0 copy-done.6
  93.1 13.3 %all-reduce.2 = (f32[]{:T(128)}, f32[384]{0:T(512)S(1)}, f32[384]{0:T(512)S(1)}) all-reduce(f32[]{:T(128)} %subtract_reduce_fusion, f32[384]{0:T(512)S(1)} %convert_dynamic-update-slice_fusion, f32[384]{0:T(512)S(1)} %copy-done.6), channel_id=1, replica_groups=mesh['dp'=8,'fsdp'=4] {'dp'}, use_global_device_ids=true, to_apply=%region_5.6 | all-reduce | flops 769 | bytes 6152 | tf_op jit(solution)/shard_map/psum | solution.py:85
  107.1 0.0 copy-done.3
  107.1 12.2 %all_gather.22 = bf16[48,1024]{1,0:T(8,128)(2,1)S(1)} all-gather(bf16[48,256]{1,0:T(8,128)(2,1)S(1)} %copy-done.3), channel_id=1, replica_groups=mesh['dp'=8,'fsdp'=4] {'fsdp'}, dimensions={1}, use_global_device_ids=true | all-gather | bytes 122880 | tf_op jit(solution)/shard_map/all_gather | solution.py:62
  119.3 0.0 copy-done
  119.3 0.7 fusion.33
  120.0 17.5 %all_gather.23 = f32[48,4096]{1,0:T(8,128)S(1)} all-gather(f32[48,1024]{1,0:T(8,128)S(1)} %fusion.33), channel_id=1, replica_groups=mesh['dp'=8,'fsdp'=4] {'fsdp'}, dimensions={1}, use_global_device_ids=true | all-gather | bytes 983040 | tf_op jit(solution)/shard_map/all_gather | solution.py:66
  137.6 0.0 copy-done.12
  137.6 0.0 copy-done.13
  137.6 0.0 copy-done.16
  137.6 0.0 copy-start.4
  137.6 0.0 copy-start.10
  137.6 2.8 %fusion.6 = (f32[4096]{0:T(1024)S(1)}, f32[128]{0:T(128)S(1)}, f32[128,4096]{1,0:T(8,128)}) fusion(bf16[128,4096]{1,0:T(8,128)(2,1)S(1)} %copy-done.1, f32[128]{0:T(128)S(1)} %copy-done.12, f32[4096]{0:T(1024)S(1)} %convert_element_type.53, f32[48,4096]{1,0:T(8,128)S(1)} %all_gather.23, f32[48]{0:T(128)S(1)} %copy-done.13, s32[128]{0:T(128)S(1)} %bitcast.13), kind=kOutput, calls=%fused_computation.11 | convolution fusion | flops 305858432 | bytes 3966656 | tf_op jit(solution)/shard_map/dot_general | solution.py:68
  140.4 42.0 %psum.46 = f32[4096]{0:T(1024)} all-reduce(f32[4096]{0:T(1024)S(1)} %get-tuple-element.6), channel_id=1, replica_groups=mesh['dp'=8,'fsdp'=4] {'dp','fsdp'}, use_global_device_ids=true, to_apply=%region_12.13 | all-reduce | flops 4096 | bytes 32768 | tf_op jit(solution)/shard_map/psum | solution.py:86
  182.5 0.0 copy-done.4
  182.5 0.8 convolution_multiply_fusion
  183.3 0.0 copy-done.10
  183.3 3.2 %fusion.3 = bf16[128,4096]{1,0:T(8,128)(2,1)} fusion(bf16[128,4096]{1,0:T(8,128)(2,1)S(1)} %copy-done.1, f32[128,4096]{1,0:T(8,128)} %get-tuple-element.22, f32[128]{0:T(128)S(1)} %broadcast_multiply_fusion, f32[128]{0:T(128)S(1)} %copy-done.10, f32[4096]{0:T(1024)S(1)} %convert_element_type.53, f32[128]{0:T(128)S(1)} %copy-done.12), kind=kLoop, calls=%fused_computation.8 | loop fusion | flops 3670016 | bytes 4212224 | tf_op jit(solution)/shard_map/convert_element_type | solution.py:78
  (6 shorter events, 0.0 us)
Async XLA Ops:
  7.2 112.1 %copy-start = (bf16[1024,1024]{1,0:T(8,128)(2,1)S(1)}, bf16[1024,1024]{1,0:T(8,128)(2,1)}, u32[]{:S(2)}) copy-start(bf16[1024,1024]{1,0:T(8,128)(2,1)} %param.13) | copy-start | bytes 6291460
  7.2 23.9 %copy-start.1 = (bf16[128,4096]{1,0:T(8,128)(2,1)S(1)}, bf16[128,4096]{1,0:T(8,128)(2,1)}, u32[]{:S(2)}) copy-start(bf16[128,4096]{1,0:T(8,128)(2,1)} %param.10) | copy-start | bytes 3145732
  7.2 75.6 %all-reduce.6.cloned.1.call-start = ((), (), s32[]{:S(2)}) async-start(), calls=%async_computation.2 | async-start | bytes 1867776 | tf_op jit(solution)/shard_map/psum | solution.py:24
  7.2 23.8 %copy-start.15 = (s32[1,128]{1,0:T(1,128)S(1)}, s32[1,128]{1,0:T(1,128)}, u32[]{:S(2)}) copy-start(s32[1,128]{1,0:T(1,128)} %param.11) | copy-start | bytes 1540
  9.5 21.5 %copy-start.11 = (f32[128]{0:T(128)}, f32[128]{0:T(128)S(1)}, u32[]{:S(2)}) copy-start(f32[128]{0:T(128)S(1)} %get-tuple-element.19) | copy-start | bytes 1540
  32.4 154.0 %reduce-scatter.2.cloned.1.call-start = ((), (), s32[]{:S(2)}) async-start(), calls=%async_computation.1 | async-start | bytes 4718592 | tf_op jit(solution)/shard_map/reduce_scatter | solution.py:79
  85.5 1.7 copy-start.5
  85.5 1.7 copy-start.8
  87.2 0.6 copy-start.2
  91.7 0.7 copy-start.7
  91.7 0.7 copy-start.9
  91.8 0.7 copy-start.14
  91.8 1.3 copy-start.6
  91.8 15.3 %copy-start.3 = (bf16[48,256]{1,0:T(8,128)(2,1)S(1)}, bf16[48,256]{1,0:T(8,128)(2,1)}, u32[]{:S(2)}) copy-start(bf16[48,256]{1,0:T(8,128)(2,1)} %copy-done.2) | copy-start | bytes 73732
  91.8 45.8 %copy-start.12 = (f32[128]{0:T(128)S(1)}, f32[128]{0:T(128)}, u32[]{:S(2)}) copy-start(f32[128]{0:T(128)} %copy-done.11) | copy-start | bytes 1540
  91.8 45.8 %copy-start.13 = (f32[48]{0:T(128)S(1)}, f32[48]{0:T(128)}, u32[]{:S(2)}) copy-start(f32[48]{0:T(128)} %psum.45) | copy-start | bytes 580
  91.8 45.8 %copy-start.16 = (s32[1,128]{1,0:T(1,128)S(1)}, s32[1,128]{1,0:T(1,128)}, u32[]{:S(2)}) copy-start(s32[1,128]{1,0:T(1,128)} %param.11) | copy-start | bytes 1540
  137.6 44.9 %copy-start.4 = (f32[48,384]{1,0:T(8,128)S(1)}, f32[48,384]{1,0:T(8,128)}, u32[]{:S(2)}) copy-start(f32[48,384]{1,0:T(8,128)} %get-tuple-element.14) | copy-start | bytes 221188
  137.6 45.7 %copy-start.10 = (f32[128]{0:T(128)S(1)}, f32[128]{0:T(128)}, u32[]{:S(2)}) copy-start(f32[128]{0:T(128)} %get-tuple-element.18) | copy-start | bytes 1540
Sparse Core Ops, SparseCore 0:
  32.6 50.2 all-reduce.5
  91.9 50.7 reduce-scatter.1
where the time goes:
time: 195 us; the launch traced here: 194 us
  blocking collectives  113 us (58%)
  waiting for transfers between devices  37.4 us (19%)
  between operations  16.6 us (9%)
  matrix products  14.5 us (7%)
  other arithmetic  10.8 us (6%)
  local copies, waits for them, and re-layouts  2.47 us (1%)
    psum x1, blocking collectives, local(): gain_grad = lax.psum(gain_part, ('dp', 'fsdp'))  42 us
    psum x1, waiting for transfers between devices, local(): scores = lax.psum(partial_value, 'fsdp') * logit_scale  37.4 us
    all_gather x1, blocking collectives, local(): mean_grad = lax.all_gather(mean_part, 'fsdp', axis=1, tiled=True)  17.5 us
    psum x1, blocking collectives, local(): loss_total = lax.psum(loss_local, 'dp')  13.3 us
    all_gather x1, blocking collectives, local(): grad_full = lax.all_gather(grad_low, 'fsdp', axis=1, tiled=True)  12.2 us
    psum x1, blocking collectives, local(): pooled, counts = lax.psum((pooled_part, counts_part), 'fsdp')  9.73 us
    all_gather x1, blocking collectives, local(): lax.all_gather(query_cache, 'dp', axis=0, tiled=True)  9.23 us
    all_gather x1, blocking collectives, local(): lax.all_gather(region_cache, 'dp', axis=0, tiled=True)  8.47 us
  transfers between devices with their start and end apart: 2, of which 1 were waited for; matrix products, arithmetic and copies ran while one was open for 6% of the time, Pallas kernels for 0%

commit v1 on v0

--- a/solution.py
+++ b/solution.py
@@ -83,7 +83,9 @@
         tiled=True,
     )
     loss_total = lax.psum(loss_local, "dp")
-    gain_grad = lax.psum(gain_part, ("dp", "fsdp"))
+    gain_grad = gain_part
+    for mesh_axis in ("fsdp", "dp"):
+        gain_grad = lax.psum(gain_grad, mesh_axis)
     mean_loss = loss_total / pair_count
     return (mean_loss, query_grad, region_grad, hidden_grad, gain_grad, proj_grad)
 

time: 195 us -> 184 us (0.944)
  the two profiles are of different devices: /device:TPU:12 before, /device:TPU:0 now
where the time goes in v1:
time: 184 us; the launch traced here: 183 us
  blocking collectives  105 us (57%)
  waiting for transfers between devices  33.7 us (18%)
  between operations  16.6 us (9%)
  matrix products  14.5 us (8%)
  other arithmetic  10.8 us (6%)
  local copies, waits for them, and re-layouts  2.5 us (1%)
    psum x1, waiting for transfers between devices, local(): scores = lax.psum(partial_value, 'fsdp') * logit_scale  33.7 us
    psum x1, blocking collectives, local(): loss_total = lax.psum(loss_local, 'dp')  23.5 us
    psum x1, blocking collectives, local(): gain_grad = lax.psum(gain_grad, mesh_axis)  17.5 us
    all_gather x1, blocking collectives, local(): mean_grad = lax.all_gather(mean_part, 'fsdp', axis=1, tiled=True)  17.1 us
    all_gather x1, blocking collectives, local(): grad_full = lax.all_gather(grad_low, 'fsdp', axis=1, tiled=True)  13.5 us
    psum x1, blocking collectives, local(): pooled, counts = lax.psum((pooled_part, counts_part), 'fsdp')  13 us
    all_gather x1, blocking collectives, local(): lax.all_gather(query_cache, 'dp', axis=0, tiled=True)  10.9 us
    all_gather x1, blocking collectives, local(): lax.all_gather(region_cache, 'dp', axis=0, tiled=True)  9.04 us
  transfers between devices with their start and end apart: 2, of which 1 were waited for; matrix products, arithmetic and copies ran while one was open for 6% of the time, Pallas kernels for 0%

profile of v1, /device:TPU:0, one launch (start us, length us, event | category | flops | bytes accessed | tf_op | source)
XLA Modules:
  0.0 182.7 jit_solution(4440469757987572090)
XLA Ops:
  7.2 0.0 copy-start
  7.2 0.0 copy-start.1
  7.2 0.0 all-reduce.6.cloned.1.call-start
  7.2 0.0 copy-start.15
  7.2 1.7 fusion
  8.9 0.6 multiply_multiply_fusion
  9.5 0.0 copy-start.11
  9.5 0.7 convert_element_type.53
  10.2 10.9 %all_gather.19 = bf16[384,256]{1,0:T(8,128)(2,1)S(1)} all-gather(bf16[48,256]{1,0:T(8,128)(2,1)} %param.7), channel_id=1, replica_groups=mesh['dp'=8,'fsdp'=4] {'dp'}, dimensions={0}, use_global_device_ids=true | all-gather | bytes 221184 | tf_op jit(solution)/shard_map/all_gather | solution.py:19
  21.1 9.0 %all_gather.18 = bf16[384,256]{1,0:T(8,128)(2,1)S(1)} all-gather(bf16[48,256]{1,0:T(8,128)(2,1)} %param.8), channel_id=1, replica_groups=mesh['dp'=8,'fsdp'=4] {'dp'}, dimensions={0}, use_global_device_ids=true | all-gather | bytes 221184 | tf_op jit(solution)/shard_map/all_gather | solution.py:18
  30.2 1.6 fusion.32
  31.7 1.6 fusion.31
  33.3 0.0 copy-done.11
  33.3 0.0 copy-done.1
  33.3 0.0 copy-done.15
  33.3 1.4 fusion.9
  34.7 0.0 all-reduce.6.cloned.1.call-update
  34.7 0.0 reduce-scatter.2.cloned.1.call-start
  34.7 1.2 dynamic-slice
  36.6 1.3 convert_reduce_fusion
  37.9 13.0 %psum.52 = f32[48]{0:T(128)} all-reduce(f32[48]{0:T(128)} %convert_reduce_fusion), channel_id=1, replica_groups=mesh['dp'=8,'fsdp'=4] {'fsdp'}, use_global_device_ids=true, to_apply=%region_9.10 | all-reduce | flops 48 | bytes 384 | tf_op jit(solution)/shard_map/psum | solution.py:59
  51.0 33.7 %all-reduce.6.cloned.1.call-done = (f32[48,384]{1,0:T(8,128)}, f32[48,384]{1,0:T(8,128)}, f32[48,4096]{1,0:T(8,128)}) async-done(((f32[48,384]{1,0:T(8,128)}, f32[48,384]{1,0:T(8,128)}, f32[48,4096]{1,0:T(8,128)}), (f32[48,384]{1,0:T(8,128)}, f32[48,384]{1,0:T(8,128)}, f32[48,4096]{1,0:T(8,128)})) %all-reduce.6.cloned.1.call-update) | async-done | bytes 933904 | tf_op jit(solution)/shard_map/psum | solution.py:24
  84.6 1.0 multiply_reduce_fusion
  85.6 1.6 select_reduce_fusion
  87.2 0.1 fusion.29
  87.3 0.0 copy-start.5
  87.3 0.0 copy-start.8
  87.3 1.7 fusion.30
  89.0 0.0 copy-done.5
  89.0 0.0 copy-start.2
  89.0 0.0 copy-done.8
  89.1 0.6 copy-done.2
  89.7 3.9 %fusion.15 = f32[4096,256]{1,0:T(8,128)} fusion(bf16[48,256]{1,0:T(8,128)(2,1)S(1)} %get-tuple-element.21, f32[48,4096]{1,0:T(8,128)} %get-tuple-element.16, f32[48]{0:T(128)} %psum.52), kind=kOutput, calls=%fused_computation.22 | convolution fusion | flops 101056512 | bytes 5005504 | tf_op jit(solution)/shard_map/dot_general | solution.py:80
  93.6 0.0 copy-start.7
  93.6 0.0 reduce-scatter.2.cloned.1.call-update
  93.6 0.0 copy-start.12
  93.6 0.0 copy-start.13
  93.6 0.0 copy-start.16
  93.6 0.6 copy-done.7
  94.2 0.1 convert_dynamic-update-slice_fusion
  94.3 0.0 copy-done.3
  94.3 13.5 %all_gather.22 = bf16[48,1024]{1,0:T(8,128)(2,1)S(1)} all-gather(bf16[48,256]{1,0:T(8,128)(2,1)S(1)} %copy-done.3), channel_id=1, replica_groups=mesh['dp'=8,'fsdp'=4] {'fsdp'}, dimensions={1}, use_global_device_ids=true | all-gather | bytes 122880 | tf_op jit(solution)/shard_map/all_gather | solution.py:62
  107.8 0.0 copy-done
  107.8 0.7 fusion.33
  108.5 17.1 %all_gather.23 = f32[48,4096]{1,0:T(8,128)S(1)} all-gather(f32[48,1024]{1,0:T(8,128)S(1)} %fusion.33), channel_id=1, replica_groups=mesh['dp'=8,'fsdp'=4] {'fsdp'}, dimensions={1}, use_global_device_ids=true | all-gather | bytes 983040 | tf_op jit(solution)/shard_map/all_gather | solution.py:66
  125.6 0.0 copy-done.12
  125.6 0.0 copy-done.13
  125.6 0.0 copy-done.16
  125.6 0.0 copy-start.9
  125.6 0.0 copy-start.14
  125.7 0.0 copy-start.6
  125.7 0.0 copy-start.4
  125.7 0.0 copy-start.10
  125.7 2.8 %fusion.6 = (f32[4096]{0:T(1024)S(1)}, f32[128]{0:T(128)S(1)}, f32[128,4096]{1,0:T(8,128)}) fusion(bf16[128,4096]{1,0:T(8,128)(2,1)S(1)} %copy-done.1, f32[128]{0:T(128)S(1)} %copy-done.12, f32[4096]{0:T(1024)S(1)} %convert_element_type.53, f32[48,4096]{1,0:T(8,128)S(1)} %all_gather.23, f32[48]{0:T(128)S(1)} %copy-done.13, s32[128]{0:T(128)S(1)} %bitcast.13), kind=kOutput, calls=%fused_computation.11 | convolution fusion | flops 305858432 | bytes 3966656 | tf_op jit(solution)/shard_map/dot_general | solution.py:68
  128.5 17.5 %psum.53 = f32[4096]{0:T(1024)S(1)} all-reduce(f32[4096]{0:T(1024)S(1)} %get-tuple-element.6), channel_id=1, replica_groups=mesh['dp'=8,'fsdp'=4] {'fsdp'}, use_global_device_ids=true, to_apply=%region_12.13 | all-reduce | flops 4096 | bytes 32768 | tf_op jit(solution)/shard_map/psum | solution.py:88
  146.0 0.0 copy-done.9
  146.0 0.0 copy-done.14
  146.0 0.6 subtract_reduce_fusion
  146.6 0.0 copy-done.6
  146.6 23.5 %all-reduce.2 = (f32[]{:T(128)}, f32[384]{0:T(512)S(1)}, f32[384]{0:T(512)S(1)}, f32[4096]{0:T(1024)}) all-reduce(f32[]{:T(128)} %subtract_reduce_fusion, f32[384]{0:T(512)S(1)} %convert_dynamic-update-slice_fusion, f32[384]{0:T(512)S(1)} %copy-done.6, f32[4096]{0:T(1024)S(1)} %psum.53), channel_id=1, replica_groups=mesh['dp'=8,'fsdp'=4] {'dp'}, use_global_device_ids=true, to_apply=%region_5.6 | all-reduce | flops 4865 | bytes 38920 | tf_op jit(solution)/shard_map/psum | solution.py:85
  170.8 0.0 copy-done.4
  170.8 0.8 convolution_multiply_fusion
  171.6 0.0 copy-done.10
  171.6 3.2 %fusion.3 = bf16[128,4096]{1,0:T(8,128)(2,1)} fusion(bf16[128,4096]{1,0:T(8,128)(2,1)S(1)} %copy-done.1, f32[128,4096]{1,0:T(8,128)} %get-tuple-element.23, f32[128]{0:T(128)S(1)} %broadcast_multiply_fusion, f32[128]{0:T(128)S(1)} %copy-done.10, f32[4096]{0:T(1024)S(1)} %convert_element_type.53, f32[128]{0:T(128)S(1)} %copy-done.12), kind=kLoop, calls=%fused_computation.8 | loop fusion | flops 3670016 | bytes 4212224 | tf_op jit(solution)/shard_map/convert_element_type | solution.py:78
  (6 shorter events, 0.0 us)
Async XLA Ops:
  7.2 100.6 %copy-start = (bf16[1024,1024]{1,0:T(8,128)(2,1)S(1)}, bf16[1024,1024]{1,0:T(8,128)(2,1)}, u32[]{:S(2)}) copy-start(bf16[1024,1024]{1,0:T(8,128)(2,1)} %param.13) | copy-start | bytes 6291460
  7.2 26.1 %copy-start.1 = (bf16[128,4096]{1,0:T(8,128)(2,1)S(1)}, bf16[128,4096]{1,0:T(8,128)(2,1)}, u32[]{:S(2)}) copy-start(bf16[128,4096]{1,0:T(8,128)(2,1)} %param.10) | copy-start | bytes 3145732
  7.2 77.4 %all-reduce.6.cloned.1.call-start = ((), (), s32[]{:S(2)}) async-start(), calls=%async_computation.2 | async-start | bytes 1867776 | tf_op jit(solution)/shard_map/psum | solution.py:24
  7.2 26.1 %copy-start.15 = (s32[1,128]{1,0:T(1,128)S(1)}, s32[1,128]{1,0:T(1,128)}, u32[]{:S(2)}) copy-start(s32[1,128]{1,0:T(1,128)} %param.11) | copy-start | bytes 1540
  9.5 23.8 %copy-start.11 = (f32[128]{0:T(128)}, f32[128]{0:T(128)S(1)}, u32[]{:S(2)}) copy-start(f32[128]{0:T(128)S(1)} %get-tuple-element.20) | copy-start | bytes 1540
  34.7 140.1 %reduce-scatter.2.cloned.1.call-start = ((), (), s32[]{:S(2)}) async-start(), calls=%async_computation.1 | async-start | bytes 4718592 | tf_op jit(solution)/shard_map/reduce_scatter | solution.py:79
  87.3 1.7 copy-start.5
  87.3 1.7 copy-start.8
  89.0 0.6 copy-start.2
  93.6 0.7 copy-start.7
  93.6 0.8 copy-start.3
  93.6 32.0 %copy-start.12 = (f32[128]{0:T(128)S(1)}, f32[128]{0:T(128)}, u32[]{:S(2)}) copy-start(f32[128]{0:T(128)} %copy-done.11) | copy-start | bytes 1540
  93.6 32.0 %copy-start.13 = (f32[48]{0:T(128)S(1)}, f32[48]{0:T(128)}, u32[]{:S(2)}) copy-start(f32[48]{0:T(128)} %psum.52) | copy-start | bytes 580
  93.6 32.0 %copy-start.16 = (s32[1,128]{1,0:T(1,128)S(1)}, s32[1,128]{1,0:T(1,128)}, u32[]{:S(2)}) copy-start(s32[1,128]{1,0:T(1,128)} %param.11) | copy-start | bytes 1540
  125.6 20.4 %copy-start.9 = (f32[48]{0:T(128)S(1)}, f32[48]{0:T(128)}, u32[]{:S(2)}) copy-start(f32[48]{0:T(128)} %copy-done.8) | copy-start | bytes 580
  125.6 20.3 %copy-start.14 = (f32[48]{0:T(128)S(1)}, f32[48]{0:T(128)}, u32[]{:S(2)}) copy-start(f32[48]{0:T(128)} %get-tuple-element.8) | copy-start | bytes 580
  125.7 20.9 %copy-start.6 = (f32[384]{0:T(512)S(1)}, f32[384]{0:T(512)}, u32[]{:S(2)}) copy-start(f32[384]{0:T(512)} %copy-done.5) | copy-start | bytes 4612
  125.7 45.1 %copy-start.4 = (f32[48,384]{1,0:T(8,128)S(1)}, f32[48,384]{1,0:T(8,128)}, u32[]{:S(2)}) copy-start(f32[48,384]{1,0:T(8,128)} %get-tuple-element.15) | copy-start | bytes 221188
  125.7 45.9 %copy-start.10 = (f32[128]{0:T(128)S(1)}, f32[128]{0:T(128)}, u32[]{:S(2)}) copy-start(f32[128]{0:T(128)} %get-tuple-element.19) | copy-start | bytes 1540
Sparse Core Ops, SparseCore 0:
  34.8 49.7 all-reduce.5
  93.7 50.6 reduce-scatter.1
